TPU v7x, 512 devices: a whole 4x4x16 slice. The times are simulated.
512 devices in a mesh: ctx: 64 (over z_lo, y, core), wa: 8 (over z_hi, x).
Axes of the slice: x: 4, y: 4, z: 16 (z_hi: 2, z_lo: 8; z = z_hi * 8 + z_lo), core: 2. Of those that a mesh axis runs over, the one named last changes fastest.
Arguments:
- q_nope: bfloat16 [512, 8192], P('ctx', 'wa'), may hold values from -6 to 6
- q_rope: bfloat16 [512, 4096], P('ctx', 'wa'), may hold values from -100 to 100
- w_uk: bfloat16 [64, 128, 512], P('wa'), may hold values from -0.25 to 0.25
- w_uv: bfloat16 [64, 512, 128], P('wa'), may hold values from -0.25 to 0.25
- cache: bfloat16 [32768, 576], P('ctx'), may hold values from -16 to 16
- cache_scale: float32 [32768], P('ctx'), may hold values from 0.5 to 2, as said below
- new_latent: bfloat16 [512, 576], P('ctx'), may hold values from -16 to 16
- cache_doc: int32 [512], P('ctx'), may hold values from 0 to 15
- new_lengths: int32 [16], replicated, may hold values from 1 to 128, 512 in all
Outputs:
- attn_out: bfloat16 [512, 8192], P('ctx', 'wa')
Inputs may be any that keep to these rules, and one draw needn't show every extreme that they name: `cache_scale`: each scale is 0.5, 1 or 2.
All inputs are finite; a program needn't handle non-finite values.
Results may differ from a plain program's by a relative error of at most 0.0064.
Values may be sent and summed in bfloat16 or wider, within the bound.
No kernel may reach another device: no remote copies, remote signals or barrier semaphores. Data moves between devices by JAX's collectives and lax.ppermute only.
A program may use at most 64 MiB of HBM per device.

v0:
```python
import jax
import jax.numpy as jnp
from jax import lax
from jax.sharding import PartitionSpec as P


def doc_index(position, new_lengths):
    ends = jnp.cumsum(new_lengths)
    return jnp.sum((ends[None, :] <= position[:, None]).astype(jnp.int32), axis=1)


def absorb_rows(nope_rows, w_uk):
    row_count = nope_rows.shape[0]
    heads_dev, nope_dim, latent_dim = w_uk.shape
    shaped = nope_rows.reshape(row_count, heads_dev, nope_dim)
    absorbed = jnp.einsum("thn,hnl->thl", shaped, w_uk, preferred_element_type=jnp.float32)
    return absorbed.astype(jnp.bfloat16)


def body(q_nope, q_rope, w_uk, w_uv, cache, cache_scale, new_latent, cache_doc, new_lengths):
    tok_rows = q_nope.shape[0]
    heads_dev, nope_dim, latent_dim = w_uk.shape
    value_dim = w_uv.shape[2]
    rope_dim = q_rope.shape[1] // heads_dev
    shards = lax.axis_size("ctx")
    all_rows = tok_rows * shards
    my_index = lax.axis_index("ctx")
    score_scale = (nope_dim + rope_dim) ** (-0.5)
    own_q = jnp.concatenate([q_nope, q_rope], axis=1)
    all_q = lax.all_gather(own_q, "ctx", axis=0, tiled=True)
    nope_width = heads_dev * nope_dim
    all_lat = absorb_rows(all_q[:, :nope_width], w_uk)
    all_rope = all_q[:, nope_width:]
    query = jnp.concatenate([all_lat, all_rope.reshape(all_rows, heads_dev, rope_dim)], axis=2)
    dequant = (cache.astype(jnp.float32) * cache_scale[:, None]).astype(jnp.bfloat16)
    key_rows = jnp.concatenate([dequant, new_latent], axis=0)
    cache_len = cache.shape[0]
    block_len = cache_len // cache_doc.shape[0]
    query_pos = jnp.arange(all_rows, dtype=jnp.int32)
    query_doc = doc_index(query_pos, new_lengths)
    new_pos = my_index * tok_rows + jnp.arange(tok_rows, dtype=jnp.int32)
    key_doc = jnp.concatenate([jnp.repeat(cache_doc, block_len), doc_index(new_pos, new_lengths)])
    key_pos = jnp.concatenate([jnp.full((cache_len,), -1, dtype=jnp.int32), new_pos])
    allowed = (query_doc[:, None] == key_doc[None, :]) & (key_pos[None, :] <= query_pos[:, None])
    score = (
        jnp.einsum("qhl,kl->qhk", query, key_rows, preferred_element_type=jnp.float32) * score_scale
    )
    masked = jnp.where(allowed[:, None, :], score, -jnp.inf)
    local_max = jnp.max(masked, axis=2)
    shift = jnp.where(jnp.isfinite(local_max), local_max, jnp.zeros_like(local_max))
    weight = jnp.exp(masked - shift[:, :, None])
    totals = jnp.sum(weight, axis=2)
    weight_low = weight.astype(jnp.bfloat16)
    part_lat = jnp.einsum(
        "qhk,kl->qhl", weight_low, key_rows[:, :latent_dim], preferred_element_type=jnp.float32
    ).astype(jnp.bfloat16)
    numerator = jnp.einsum("qhl,hlv->qhv", part_lat, w_uv, preferred_element_type=jnp.float32)
    stats = lax.all_gather(jnp.concatenate([local_max, totals], axis=1), "ctx", axis=0, tiled=False)
    row_max = jnp.max(stats[:, :, :heads_dev], axis=0)
    factor = jnp.exp(local_max - row_max)
    scaled = (numerator * factor[:, :, None]).reshape(all_rows, heads_dev * value_dim)
    own_numer = lax.psum_scatter(scaled, "ctx", scatter_dimension=0, tiled=True)
    own_numer = own_numer.reshape(tok_rows, heads_dev, value_dim)
    own_stats = lax.dynamic_slice_in_dim(stats, my_index * tok_rows, tok_rows, axis=1)
    own_max = lax.dynamic_slice_in_dim(row_max, my_index * tok_rows, tok_rows, axis=0)
    own_factor = jnp.exp(own_stats[:, :, :heads_dev] - own_max[None])
    own_total = jnp.sum(own_factor * own_stats[:, :, heads_dev:], axis=0)
    result = own_numer / own_total[:, :, None]
    return result.astype(jnp.bfloat16).reshape(tok_rows, heads_dev * value_dim)


def solution(mesh):
    placed = (
        P("ctx", "wa"),
        P("ctx", "wa"),
        P("wa", None, None),
        P("wa", None, None),
        P("ctx", None),
        P("ctx"),
        P("ctx", None),
        P("ctx"),
        P(),
    )
    return jax.shard_map(
        body, mesh=mesh, in_specs=placed, out_specs=P("ctx", "wa"), check_vma=False
    )
```

profile of v0, /device:TPU:2, one launch (start us, length us, event | category | flops | bytes accessed | tf_op | source)
XLA Modules:
  0.0 727.8 jit_solution(12860980277982599046)
XLA Ops:
  6.5 0.0 copy-start
  6.5 0.0 all-gather.4.cloned.1.call-start
  6.5 1.4 pad_maximum_fusion.2
  8.0 0.0 all-gather.4.cloned.1.call-update
  8.0 0.0 all-gather.6.cloned.1.call-start
  8.0 0.7 copy.42
  8.8 0.1 reduce
  8.9 0.7 broadcast_in_dim.12
  9.7 0.1 reshape.99
  9.7 1.5 copy.47
  11.2 0.2 convert_reduce_fusion.1
  11.4 0.1 convert_reduce_fusion
  11.5 0.3 fusion.23
  11.8 2.0 multiply_convert_fusion
  13.8 120.8 %all-gather.4.cloned.1.call-done = bf16[512,1536]{1,0:T(8,128)(2,1)} async-done(((bf16[8,1536]{1,0:T(8,128)(2,1)}), bf16[512,1536]{1,0:T(8,128)(2,1)}) %all-gather.4.cloned.1.call-update) | async-done | bytes 1572880 | tf_op jit(solution)/shard_map/all_gather | solution.py:30
  134.6 1.3 slice.24
  135.9 0.5 copy.59
  136.5 0.0 copy-start.4
  136.5 1.1 slice.25
  137.6 1.0 copy.46
  138.6 0.0 copy-start.2
  138.6 0.0 copy-start.3
  138.6 0.0 copy-done
  138.6 1.3 convert_bitcast_fusion
  139.9 0.0 copy-done.4
  139.9 0.0 copy-done.2
  139.9 0.0 copy-done.3
  140.0 4.7 fusion
  144.6 0.0 copy-start.1
  144.7 1.7 fusion.1
  146.4 1.5 copy-done.1
  147.9 0.6 pad_maximum_fusion.1
  148.5 0.0 all-gather.6.cloned.1.call-update
  148.6 0.2 reduce-scatter.2.cloned.1.call-start
  148.8 116.5 %all-gather.6.cloned.1.call-done = f32[32768,16]{0,1:T(8,128)} async-done(((f32[512,16]{0,1:T(8,128)}), f32[32768,16]{0,1:T(8,128)}) %all-gather.6.cloned.1.call-update) | async-done | bytes 2097168 | tf_op jit(solution)/shard_map/all_gather | solution.py:58
  265.3 2.8 copy.60
  268.1 0.1 slice_reduce_fusion
  268.2 10.4 %bitcast_multiply_fusion = f32[512,8,128]{0,2,1:T(8,128)} fusion(bf16[8,512,128]{2,1,0:T(8,128)(2,1)} %param.12, f32[512,8,520]{0,2,1:T(8,128)} %copy-done.1, f32[512,8]{0,1:T(8,128)S(1)} %is-finite_select_fusion, pred[512,520]{0,1:T(8,128)(4,1)S(1)} %fusion.23, f32[512,8]{0,1:T(8,128)S(1)} %subtract_exponential_fusion.1, ...), kind=kOutput, calls=%fused_computation.17 | convolution fusion | flops 2730115072 | bytes 12563456 | tf_op jit(solution)/shard_map/qhl,hlv->qhv/dot_general | solution.py:57
  278.6 2.9 copy.51
  281.5 0.0 reduce-scatter.2.cloned.1.call-update
  281.5 0.1 constant_dynamic-slice_fusion
  281.6 0.2 fusion.31
  281.8 438.0 %reduce-scatter.2.cloned.1.call-done = f32[8,1024]{1,0:T(8,128)} async-done(((f32[512,1024]{1,0:T(8,128)}), f32[8,1024]{1,0:T(8,128)}) %reduce-scatter.2.cloned.1.call-update) | async-done | bytes 32784 | tf_op jit(solution)/shard_map/reduce_scatter | solution.py:62
  719.8 1.4 fusion.33
  (6 shorter events, 0.1 us)
Async XLA Ops:
  6.5 132.1 %copy-start = (bf16[8,128,512]{2,1,0:T(8,128)(2,1)S(1)}, bf16[8,128,512]{2,1,0:T(8,128)(2,1)}, u32[]{:S(2)}) copy-start(bf16[8,128,512]{2,1,0:T(8,128)(2,1)} %param.11) | copy-start | bytes 3145732
  6.5 128.1 %all-gather.4.cloned.1.call-start = ((), (), s32[]{:S(2)}) async-start(), calls=%async_computation.1 | async-start | bytes 1597440 | tf_op jit(solution)/shard_map/all_gather | solution.py:30
  8.0 257.3 %all-gather.6.cloned.1.call-start = ((), (), s32[]{:S(2)}) async-start(), calls=%async_computation.3 | async-start | bytes 2129920 | tf_op jit(solution)/shard_map/all_gather | solution.py:58
  136.5 3.4 copy-start.4
  138.6 1.3 copy-start.2
  138.6 1.3 copy-start.3
  144.6 3.3 copy-start.1
  148.6 571.3 %reduce-scatter.2.cloned.1.call-start = ((), (), s32[]{:S(2)}) async-start(), calls=%async_computation.2 | async-start | bytes 2129920 | tf_op jit(solution)/shard_map/reduce_scatter | solution.py:62
Sparse Core Ops, SparseCore 0:
  9.5 125.1 all-gather.3
  148.7 116.5 all-gather.5
  281.7 438.1 reduce-scatter.1
where the time goes:
time: 728 us
  waiting for transfers between devices  675 us (93%)
  matrix products  16.3 us (2%)
  local copies, waits for them, and re-layouts  14.3 us (2%)
  between operations  13.2 us (2%)
  other arithmetic  8.3 us (1%)
    reduce_scatter x1, waiting for transfers between devices, body(): own_numer = lax.psum_scatter(scaled, 'ctx', scatter_dimension=0, tiled=True)  438 us
    all_gather x1, waiting for transfers between devices, body(): all_q = lax.all_gather(own_q, 'ctx', axis=0, tiled=True)  121 us
    all_gather x1, waiting for transfers between devices, body(): lax.all_gather(jnp.concatenate([local_max, totals], axis=1), 'ctx', axis=...  116 us
  transfers between devices with their start and end apart: 3, of which 3 were waited for; matrix products, arithmetic and copies ran while one was open for 1% of the time, Pallas kernels for 0%

commit v1 on v0

--- a/solution.py
+++ b/solution.py
@@ -27,7 +27,9 @@
     my_index = lax.axis_index("ctx")
     score_scale = (nope_dim + rope_dim) ** (-0.5)
     own_q = jnp.concatenate([q_nope, q_rope], axis=1)
-    all_q = lax.all_gather(own_q, "ctx", axis=0, tiled=True)
+    all_q = jnp.concatenate(
+        lax.all_to_all(jnp.stack([own_q] * lax.axis_size("ctx")), "ctx", 0, 0), axis=0
+    )
     nope_width = heads_dev * nope_dim
     all_lat = absorb_rows(all_q[:, :nope_width], w_uk)
     all_rope = all_q[:, nope_width:]

time: 728 us -> 694 us (0.953)
  waiting for transfers between devices: 675 us -> 626 us
  starting transfers between devices: 0.27 us -> 16.4 us
    all_gather x1 -> x0, waiting for transfers between devices: 121 us -> none  [body(): all_q = lax.all_gather(own_q, 'ctx', axis=0, tiled=True)]
    all_to_all x0 -> x1, waiting for transfers between devices: none -> 70 us  [body(): lax.all_to_all(jnp.stack([own_q] * lax.axis_size('ctx')), 'ctx', 0, 0)]
    all_to_all x0 -> x1, starting transfers between devices: none -> 16.2 us  [body(): lax.all_to_all(jnp.stack([own_q] * lax.axis_size('ctx')), 'ctx', 0, 0)]
where the time goes in v1:
time: 694 us; the launch traced here: 693 us
  waiting for transfers between devices  626 us (90%)
  matrix products  17.4 us (3%)
  starting transfers between devices  16.4 us (2%)
  between operations  13.6 us (2%)
  local copies, waits for them, and re-layouts  12.5 us (2%)
  other arithmetic  7.7 us (1%)
    reduce_scatter x1, waiting for transfers between devices, body(): own_numer = lax.psum_scatter(scaled, 'ctx', scatter_dimension=0, tiled=True)  438 us
    all_gather x1, waiting for transfers between devices, body(): lax.all_gather(jnp.concatenate([local_max, totals], axis=1), 'ctx', axis=...  118 us
    all_to_all x1, waiting for transfers between devices, body(): lax.all_to_all(jnp.stack([own_q] * lax.axis_size('ctx')), 'ctx', 0, 0)  70 us
    all_to_all x1, starting transfers between devices, body(): lax.all_to_all(jnp.stack([own_q] * lax.axis_size('ctx')), 'ctx', 0, 0)  16.2 us
  transfers between devices with their start and end apart: 3, of which 3 were waited for; matrix products, arithmetic and copies ran while one was open for 1% of the time, Pallas kernels for 0%

profile of v1, /device:TPU:2, one launch (start us, length us, event | category | flops | bytes accessed | tf_op | source)
XLA Modules:
  0.0 693.2 jit_solution(643382706939654967)
XLA Ops:
  6.5 0.0 copy-start
  6.5 0.0 copy-start.5
  6.5 0.0 copy-start.6
  6.5 0.0 copy-start.3
  6.5 0.0 copy-start.4
  6.5 0.8 pad_maximum_fusion.2
  7.4 1.3 stack.2
  8.6 16.2 %all-to-all-start = ((bf16[64,8,1536]{2,1,0:T(8,128)(2,1)}), bf16[64,8,1536]{2,1,0:T(8,128)(2,1)S(1)}, u32[]{:S(2)}, u32[]{:S(2)}) async-start(bf16[64,8,1536]{2,1,0:T(8,128)(2,1)} %stack.2), calls=%async_computation | async-start | bytes 3145728 | tf_op jit(solution)/shard_map/all_to_all | solution.py:31
  24.8 0.0 all-gather.3.cloned.1.call-start
  24.9 0.0 copy-done.5
  24.9 0.1 copy.34
  25.0 0.1 reduce
  25.1 0.0 copy-done.6
  25.1 0.1 broadcast_in_dim.12
  25.2 0.1 reshape.104
  25.3 0.0 copy-done.3
  25.3 0.8 copy.39
  26.1 0.2 convert_reduce_fusion.1
  26.3 0.1 convert_reduce_fusion
  26.3 0.3 fusion.23
  26.6 0.0 copy-done.4
  26.7 2.0 multiply_convert_fusion
  28.7 70.0 %all-to-all-done = bf16[64,8,1536]{2,1,0:T(8,128)(2,1)S(1)} async-done(((bf16[64,8,1536]{2,1,0:T(8,128)(2,1)}), bf16[64,8,1536]{2,1,0:T(8,128)(2,1)S(1)}, u32[]{:S(2)}, u32[]{:S(2)}) %all-to-all-start) | async-done | bytes 1572896 | tf_op jit(solution)/shard_map/all_to_all | solution.py:31
  98.6 1.1 slice.24
  99.8 1.5 copy.35
  101.3 0.2 copy.38
  101.5 0.0 copy-start.2
  101.5 0.0 copy-done
  101.5 1.3 convert_bitcast_fusion
  102.8 0.0 copy-done.2
  102.8 5.7 fusion
  108.6 0.0 copy-start.1
  108.6 1.7 fusion.1
  110.3 1.5 copy-done.1
  111.8 0.6 pad_maximum_fusion.1
  112.5 0.0 all-gather.3.cloned.1.call-update
  112.5 0.2 reduce-scatter.2.cloned.1.call-start
  112.7 117.7 %all-gather.3.cloned.1.call-done = f32[32768,16]{0,1:T(8,128)} async-done(((f32[512,16]{0,1:T(8,128)}), f32[32768,16]{0,1:T(8,128)}) %all-gather.3.cloned.1.call-update) | async-done | bytes 2097168 | tf_op jit(solution)/shard_map/all_gather | solution.py:60
  230.4 2.8 copy.51
  233.2 0.1 slice_reduce_fusion
  233.3 10.4 %bitcast_multiply_fusion = f32[512,8,128]{0,2,1:T(8,128)} fusion(bf16[8,512,128]{2,1,0:T(8,128)(2,1)} %param.12, f32[512,8,520]{0,2,1:T(8,128)} %copy-done.1, f32[512,8]{0,1:T(8,128)S(1)} %is-finite_select_fusion, pred[512,520]{0,1:T(8,128)(4,1)S(1)} %fusion.23, f32[512,8]{0,1:T(8,128)S(1)} %subtract_exponential_fusion.1, ...), kind=kOutput, calls=%fused_computation.17 | convolution fusion | flops 2730115072 | bytes 12563456 | tf_op jit(solution)/shard_map/qhl,hlv->qhv/dot_general | solution.py:59
  243.7 2.9 copy.43
  246.6 0.0 reduce-scatter.2.cloned.1.call-update
  246.7 0.1 constant_dynamic-slice_fusion
  246.7 0.2 fusion.31
  247.0 437.9 %reduce-scatter.2.cloned.1.call-done = f32[8,1024]{1,0:T(8,128)} async-done(((f32[512,1024]{1,0:T(8,128)}), f32[8,1024]{1,0:T(8,128)}) %reduce-scatter.2.cloned.1.call-update) | async-done | bytes 32784 | tf_op jit(solution)/shard_map/reduce_scatter | solution.py:64
  684.9 1.4 fusion.33
  (7 shorter events, 0.1 us)
Async XLA Ops:
  6.5 95.0 %copy-start = (bf16[8,128,512]{2,1,0:T(8,128)(2,1)S(1)}, bf16[8,128,512]{2,1,0:T(8,128)(2,1)}, u32[]{:S(2)}) copy-start(bf16[8,128,512]{2,1,0:T(8,128)(2,1)} %param.11) | copy-start | bytes 3145732
  6.5 18.3 %copy-start.5 = (s32[16]{0:T(128)S(1)}, s32[16]{0:T(128)}, u32[]{:S(2)}) copy-start(s32[16]{0:T(128)} %param.17) | copy-start | bytes 196
  6.5 18.6 %copy-start.6 = (s32[8]{0:T(128)S(1)}, s32[8]{0:T(128)}, u32[]{:S(2)}) copy-start(s32[8]{0:T(128)} %param.16) | copy-start | bytes 100
  6.5 18.7 %copy-start.3 = (bf16[8,576]{1,0:T(8,128)(2,1)S(1)}, bf16[8,576]{1,0:T(8,128)(2,1)}, u32[]{:S(2)}) copy-start(bf16[8,576]{1,0:T(8,128)(2,1)} %param.15) | copy-start | bytes 27652
  6.5 20.1 %copy-start.4 = (f32[512]{0:T(512)S(1)}, f32[512]{0:T(512)}, u32[]{:S(2)}) copy-start(f32[512]{0:T(512)} %param.14) | copy-start | bytes 6148
  8.6 90.0 %all-to-all-start = ((bf16[64,8,1536]{2,1,0:T(8,128)(2,1)}), bf16[64,8,1536]{2,1,0:T(8,128)(2,1)S(1)}, u32[]{:S(2)}, u32[]{:S(2)}) async-start(bf16[64,8,1536]{2,1,0:T(8,128)(2,1)} %stack.2), calls=%async_computation | async-start | bytes 3145728 | tf_op jit(solution)/shard_map/all_to_all | solution.py:31
  24.8 205.6 %all-gather.3.cloned.1.call-start = ((), (), s32[]{:S(2)}) async-start(), calls=%async_computation.3 | async-start | bytes 2129920 | tf_op jit(solution)/shard_map/all_gather | solution.py:60
  101.5 1.3 copy-start.2
  108.6 3.3 copy-start.1
  112.5 572.4 %reduce-scatter.2.cloned.1.call-start = ((), (), s32[]{:S(2)}) async-start(), calls=%async_computation.2 | async-start | bytes 2129920 | tf_op jit(solution)/shard_map/reduce_scatter | solution.py:64
Sparse Core Ops, SparseCore 0:
  112.6 117.7 all-gather.2
  246.8 438.0 reduce-scatter.1
